TPU v7x, 512 devices: a whole 4x8x8 slice. The times are simulated.
512 devices in a mesh: row: 16 (over y, x_lo), col: 16 (over z, core), ka: 2 (over x_hi).
Axes of the slice: x: 4 (x_hi: 2, x_lo: 2; x = x_hi * 2 + x_lo), y: 8, z: 8, core: 2. Of those that a mesh axis runs over, the one named last changes fastest.
Arguments:
- pair: bfloat16 [512, 512, 128], P('row', ('col', 'ka')), may hold values from -6 to 6
- pair_mask: int32 [512, 512], P('row', ('col', 'ka')), may hold values from 0 to 1, as said below
- w_in: bfloat16 [2, 128, 512], replicated, may hold values from -0.5 to 0.5
- w_gate: bfloat16 [2, 128, 128], replicated, may hold values from -0.5 to 0.5
- w_out: bfloat16 [2, 128, 128], replicated, may hold values from -0.5 to 0.5
Outputs:
- updated: bfloat16 [512, 512, 128], P('row', ('col', 'ka'))
Inputs may be any that keep to these rules, and one draw needn't show every extreme that they name: pair_mask[i, j] = v[i] v[j] for a per-token 0/1 validity v; within each aligned run of 16 tokens the real tokens come first and there is at least one.
All inputs are finite; a program needn't handle non-finite values.
Results may differ from a plain program's by a relative error of at most 0.014.
Values may be sent and summed in bfloat16 or wider, within the bound.
No kernel may reach another device: no remote copies, remote signals or barrier semaphores. Data moves between devices by JAX's collectives and lax.ppermute only.
A program may use at most 64 MiB of HBM per device.

v0:
```python
import jax
import jax.numpy as jnp
from jax import lax
from jax.sharding import PartitionSpec as P


def layer_norm(value):
    mean = jnp.mean(value, axis=-1, keepdims=True)
    centred = value - mean
    var = jnp.mean(centred * centred, axis=-1, keepdims=True)
    return centred / jnp.sqrt(var + 1e-05)


def prepare(pair, valid, weight_in, weight_gate):
    normed = layer_norm(pair.astype(jnp.float32)).astype(jnp.bfloat16)
    proj = jnp.einsum("ijc,cd->ijd", normed, weight_in, preferred_element_type=jnp.float32)
    width = proj.shape[-1] // 4
    left = (jax.nn.sigmoid(proj[..., :width]) * proj[..., width : 2 * width] * valid).astype(
        jnp.bfloat16
    )
    right = (
        jax.nn.sigmoid(proj[..., 2 * width : 3 * width]) * proj[..., 3 * width :] * valid
    ).astype(jnp.bfloat16)
    gate = jax.nn.sigmoid(
        jnp.einsum("ijc,cd->ijd", normed, weight_gate, preferred_element_type=jnp.float32)
    )
    return (left, right, gate)


def finish(pair, tri, gate, weight_out):
    normed = layer_norm(tri).astype(jnp.bfloat16)
    proj = jnp.einsum("ijc,cd->ijd", normed, weight_out, preferred_element_type=jnp.float32)
    return (pair.astype(jnp.float32) + gate * proj).astype(jnp.bfloat16)


def transpose_tiles(value, n):
    perm = [(r * n + c, c * n + r) for r in range(n) for c in range(n)]
    return lax.ppermute(value, ("row", "col"), perm)


def on_device(n, pair, pair_mask, w_in, w_gate, w_out):
    valid = pair_mask.astype(jnp.float32)[..., None]
    left, right, gate = prepare(pair, valid, w_in[0], w_gate[0])
    left_rows = lax.all_gather(left, "col", axis=1, tiled=True)
    right_diag = lax.all_gather(transpose_tiles(right, n), "row", axis=1, tiled=True)
    partial_value = jnp.einsum(
        "ikc,jkc->ijc", left_rows, right_diag, preferred_element_type=jnp.float32
    )
    tri = lax.psum_scatter(
        partial_value.astype(jnp.bfloat16), "ka", scatter_dimension=1, tiled=True
    ).astype(jnp.float32)
    middle = finish(pair, tri, gate, w_out[0])
    left, right, gate = prepare(middle, valid, w_in[1], w_gate[1])
    right_cols = lax.all_gather(right, "row", axis=0, tiled=True)
    left_half = lax.all_gather(transpose_tiles(left, n), "col", axis=0, tiled=True)
    left_diag = lax.all_gather(left_half, "ka", axis=1, tiled=True)
    tri = jnp.einsum("kic,kjc->ijc", left_diag, right_cols, preferred_element_type=jnp.float32)
    return finish(middle, tri, gate, w_out[1])


def solution(mesh):
    n = mesh.shape["row"]
    assert mesh.shape["col"] == n
    placed = (P("row", ("col", "ka"), None), P("row", ("col", "ka")), P(), P(), P())
    return jax.shard_map(
        lambda *a: on_device(n, *a),
        mesh=mesh,
        in_specs=placed,
        out_specs=P("row", ("col", "ka"), None),
        check_vma=False,
    )
```

profile of v0, /device:TPU:1, one launch (start us, length us, event | category | flops | bytes accessed | tf_op | source)
XLA Modules:
  0.0 423.1 jit_solution(14155994391619889289)
XLA Ops:
  6.5 1.0 convert_reduce_fusion.1
  7.7 1.1 fusion.18
  9.8 1.3 fusion.42
  12.1 4.5 %collective-permute-start = (bf16[32,16,128]{2,1,0:T(8,128)(2,1)S(1)}, bf16[32,16,128]{2,1,0:T(8,128)(2,1)S(1)}, u32[]{:S(2)}, u32[]{:S(2)}) collective-permute-start(bf16[32,16,128]{2,1,0:T(8,128)(2,1)S(1)} %get-tuple-element.8), channel_id=1, source_target_pairs={{0,0},{2,32},{4,64},{6,96},{8,128},{10,160},{12,192},{14,224},{16,... | collective-permute-start | bytes 393224 | tf_op jit(solution)/shard_map/ppermute | solution.py:38
  16.6 2.6 collective-permute-done
  19.9 45.1 %all-gather.8.cloned.1.call-done = bf16[32,256,128]{2,1,0:T(8,128)(2,1)} async-done(((bf16[32,16,128]{2,1,0:T(8,128)(2,1)}), bf16[32,256,128]{2,1,0:T(8,128)(2,1)}) %all-gather.8.cloned.1.call-update) | async-done | bytes 2097168 | tf_op jit(solution)/shard_map/all_gather | solution.py:44
  65.1 15.2 %copy.49 = bf16[32,256,128]{0,1,2:T(8,128)(2,1)} copy(bf16[32,256,128]{2,1,0:T(8,128)(2,1)} %all-gather.8.cloned.1.call-done) | data formatting | bytes 4194304 | tf_op jit(solution)/shard_map/all_gather | solution.py:44
  80.3 57.6 %all-gather.6.cloned.1.call-done = bf16[32,256,128]{2,1,0:T(8,128)(2,1)} async-done(((bf16[32,16,128]{2,1,0:T(8,128)(2,1)}), bf16[32,256,128]{2,1,0:T(8,128)(2,1)}) %all-gather.6.cloned.1.call-update) | async-done | bytes 2097168 | tf_op jit(solution)/shard_map/all_gather | solution.py:45
  137.9 15.2 %copy.48 = bf16[32,256,128]{0,1,2:T(8,128)(2,1)} copy(bf16[32,256,128]{2,1,0:T(8,128)(2,1)} %all-gather.6.cloned.1.call-done) | data formatting | bytes 4194304 | tf_op jit(solution)/shard_map/all_gather | solution.py:45
  153.2 9.2 %fusion = bf16[32,32,128]{0,1,2:T(8,128)(2,1)} fusion(bf16[32,256,128]{0,1,2:T(8,128)(2,1)} %copy.48, bf16[32,256,128]{0,1,2:T(8,128)(2,1)} %copy.49), kind=kOutput, calls=%fused_computation.1 | convolution fusion | flops 67239936 | bytes 4456448 | tf_op jit(solution)/shard_map/ikc,jkc->ijc/dot_general | solution.py:46
  162.8 39.5 %reduce-scatter.2.cloned.1.call-done = bf16[32,16,128]{0,1,2:T(8,128)(2,1)} async-done(((bf16[32,32,128]{0,1,2:T(8,128)(2,1)}), bf16[32,16,128]{0,1,2:T(8,128)(2,1)}) %reduce-scatter.2.cloned.1.call-update) | async-done | bytes 131088 | tf_op jit(solution)/shard_map/reduce_scatter | solution.py:49
  202.3 1.2 convert_reduce_fusion
  203.5 1.3 fusion.14
  204.8 1.2 fusion.15
  207.7 0.8 fusion.21
  208.5 2.9 collective-permute-start.1
  211.4 3.4 collective-permute-done.1
  216.1 53.4 %all-gather.12.cloned.1.call-done = bf16[512,16,128]{2,1,0:T(8,128)(2,1)} async-done(((bf16[32,16,128]{2,1,0:T(8,128)(2,1)}), bf16[512,16,128]{2,1,0:T(8,128)(2,1)}) %all-gather.12.cloned.1.call-update) | async-done | bytes 2097168 | tf_op jit(solution)/shard_map/all_gather | solution.py:55
  269.5 4.9 %copy.55 = bf16[512,16,128]{0,1,2:T(8,128)(2,1)} copy(bf16[512,16,128]{2,1,0:T(8,128)(2,1)} %all-gather.12.cloned.1.call-done) | data formatting | bytes 4194304 | tf_op jit(solution)/shard_map/all_gather | solution.py:55
  274.8 59.3 %all-gather.10.cloned.1.call-done = bf16[512,16,128]{2,1,0:T(8,128)(2,1)} async-done(((bf16[32,16,128]{2,1,0:T(8,128)(2,1)}), bf16[512,16,128]{2,1,0:T(8,128)(2,1)}) %all-gather.10.cloned.1.call-update) | async-done | bytes 2097168 | tf_op jit(solution)/shard_map/all_gather | solution.py:54
  334.1 3.9 copy.56
  338.0 73.1 %all-gather.14.cloned.1.call-done = bf16[512,32,128]{0,1,2:T(8,128)(2,1)} async-done(((bf16[512,16,128]{0,1,2:T(8,128)(2,1)}), bf16[512,32,128]{0,1,2:T(8,128)(2,1)}) %all-gather.14.cloned.1.call-update) | async-done | bytes 4194320 | tf_op jit(solution)/shard_map/all_gather | solution.py:56
  411.1 3.4 fusion.57
  415.4 0.8 fusion.13
  (52 shorter events, 7.3 us)
Async XLA Ops:
  6.5 58.5 %all-gather.8.cloned.1.call-start = ((), (), s32[]{:S(2)}) async-start(), calls=%async_computation.2 | async-start | bytes 2228224 | tf_op jit(solution)/shard_map/all_gather | solution.py:44
  12.0 125.9 %all-gather.6.cloned.1.call-start = ((), (), s32[]{:S(2)}) async-start(), calls=%async_computation.1 | async-start | bytes 2228224 | tf_op jit(solution)/shard_map/all_gather | solution.py:45
  12.1 7.1 %collective-permute-start = (bf16[32,16,128]{2,1,0:T(8,128)(2,1)S(1)}, bf16[32,16,128]{2,1,0:T(8,128)(2,1)S(1)}, u32[]{:S(2)}, u32[]{:S(2)}) collective-permute-start(bf16[32,16,128]{2,1,0:T(8,128)(2,1)S(1)} %get-tuple-element.8), channel_id=1, source_target_pairs={{0,0},{2,32},{4,64},{6,96},{8,128},{10,160},{12,192},{14,224},{16,... | collective-permute-start | bytes 393224 | tf_op jit(solution)/shard_map/ppermute | solution.py:38
  19.2 0.7 copy-start.3
  19.9 182.4 %reduce-scatter.2.cloned.1.call-start = ((), (), s32[]{:S(2)}) async-start(), calls=%async_computation.3 | async-start | bytes 1572864 | tf_op jit(solution)/shard_map/reduce_scatter | solution.py:49
  153.2 9.3 %copy-start = (bf16[32,16,128]{2,1,0:T(8,128)(2,1)S(1)}, bf16[32,16,128]{2,1,0:T(8,128)(2,1)}, u32[]{:S(2)}) copy-start(bf16[32,16,128]{2,1,0:T(8,128)(2,1)} %param.5) | copy-start | bytes 393220
  153.2 9.3 %copy-start.5 = (bf16[2,128,128]{2,1,0:T(8,128)(2,1)S(1)}, bf16[2,128,128]{2,1,0:T(8,128)(2,1)}, u32[]{:S(2)}) copy-start(bf16[2,128,128]{2,1,0:T(8,128)(2,1)} %param.8) | copy-start | bytes 196612
  162.3 44.1 %copy-start.4 = (bf16[2,128,128]{2,1,0:T(8,128)(2,1)S(1)}, bf16[2,128,128]{2,1,0:T(8,128)(2,1)}, u32[]{:S(2)}) copy-start(bf16[2,128,128]{2,1,0:T(8,128)(2,1)} %param.9) | copy-start | bytes 196612
  162.3 45.0 %copy-start.1 = (bf16[2,128,512]{2,1,0:T(8,128)(2,1)S(1)}, bf16[2,128,512]{2,1,0:T(8,128)(2,1)}, u32[]{:S(2)}) copy-start(bf16[2,128,512]{2,1,0:T(8,128)(2,1)} %param.7) | copy-start | bytes 786436
  162.4 107.2 %all-gather.12.cloned.1.call-start = ((), (), s32[]{:S(2)}) async-start(), calls=%async_computation.5 | async-start | bytes 2228224 | tf_op jit(solution)/shard_map/all_gather | solution.py:55
  208.5 6.3 %collective-permute-start.1 = (bf16[32,16,128]{2,1,0:T(8,128)(2,1)S(1)}, bf16[32,16,128]{2,1,0:T(8,128)(2,1)S(1)}, u32[]{:S(2)}, u32[]{:S(2)}) collective-permute-start(bf16[32,16,128]{2,1,0:T(8,128)(2,1)S(1)} %get-tuple-element.5), channel_id=1, source_target_pairs={{0,0},{2,32},{4,64},{6,96},{8,128},{10,160},{12,192},{14,224},{16,... | collective-permute-start | bytes 393224 | tf_op jit(solution)/shard_map/ppermute | solution.py:38
  214.8 0.6 copy-start.2
  215.5 118.6 %all-gather.10.cloned.1.call-start = ((), (), s32[]{:S(2)}) async-start(), calls=%async_computation.4 | async-start | bytes 2228224 | tf_op jit(solution)/shard_map/all_gather | solution.py:54
  216.1 195.1 %all-gather.14.cloned.1.call-start = ((), (), s32[]{:S(2)}) async-start(), calls=%async_computation.6 | async-start | bytes 6291456 | tf_op jit(solution)/shard_map/all_gather | solution.py:56
Sparse Core Ops, SparseCore 0:
  12.1 52.8 all-gather.7
  67.1 70.8 all-gather.5
  162.5 39.7 reduce-scatter.1
  215.6 53.8 all-gather.11
  271.5 62.6 all-gather.9
  336.1 75.0 all-gather.13
where the time goes:
time: 424 us; the launch traced here: 423 us
  waiting for transfers between devices  335 us (79%)
  local copies, waits for them, and re-layouts  42.3 us (10%)
  matrix products  16 us (4%)
  between operations  13.6 us (3%)
  other arithmetic  8.84 us (2%)
  starting transfers between devices  7.61 us (2%)
    all_gather x1, waiting for transfers between devices, on_device(): left_diag = lax.all_gather(left_half, 'ka', axis=1, tiled=True)  73.1 us
    all_gather x1, waiting for transfers between devices, on_device(): right_cols = lax.all_gather(right, 'row', axis=0, tiled=True)  59.3 us
    all_gather x1, waiting for transfers between devices, on_device(): lax.all_gather(transpose_tiles(right, n), 'row', axis=1, tiled=True)  57.6 us
    all_gather x1, waiting for transfers between devices, on_device(): lax.all_gather(transpose_tiles(left, n), 'col', axis=0, tiled=True)  53.4 us
    all_gather x1, waiting for transfers between devices, on_device(): left_rows = lax.all_gather(left, 'col', axis=1, tiled=True)  45.1 us
    reduce_scatter x1, waiting for transfers between devices, on_device(): lax.psum_scatter(partial_value.astype(jnp.bfloat16), 'ka', scatter_dimens...  39.5 us
    all_gather x1, local copies, waits for them, and re-layouts, on_device(): left_rows = lax.all_gather(left, 'col', axis=1, tiled=True)  15.2 us
    all_gather x1, local copies, waits for them, and re-layouts, on_device(): lax.all_gather(transpose_tiles(right, n), 'row', axis=1, tiled=True)  15.2 us
  transfers between devices with their start and end apart: 8, of which 8 were waited for; matrix products, arithmetic and copies ran while one was open for 6% of the time, Pallas kernels for 0%

commit v1 on v0

--- a/solution.py
+++ b/solution.py
@@ -41,11 +41,38 @@
 def on_device(n, pair, pair_mask, w_in, w_gate, w_out):
     valid = pair_mask.astype(jnp.float32)[..., None]
     left, right, gate = prepare(pair, valid, w_in[0], w_gate[0])
-    left_rows = lax.all_gather(left, "col", axis=1, tiled=True)
     right_diag = lax.all_gather(transpose_tiles(right, n), "row", axis=1, tiled=True)
+    length, place, rows = (lax.axis_size("col"), lax.axis_index("col"), left.shape[1])
+    ahead = [(i, (i + 1) % length) for i in range(length)]
+    backward = [(i, (i - 1) % length) for i in range(length)]
+    half = length // 2
+    from_left = from_right = left
     partial_value = jnp.einsum(
-        "ikc,jkc->ijc", left_rows, right_diag, preferred_element_type=jnp.float32
+        "ikc,jkc->ijc",
+        left,
+        lax.dynamic_slice_in_dim(right_diag, place * rows, left.shape[1], axis=1),
+        preferred_element_type=jnp.float32,
     )
+    for step in range(1, half + 1):
+        from_left = lax.ppermute(from_left, "col", ahead)
+        if step < length - half:
+            from_right = lax.ppermute(from_right, "col", backward)
+            partial_value = partial_value + jnp.einsum(
+                "ikc,jkc->ijc",
+                from_right,
+                lax.dynamic_slice_in_dim(
+                    right_diag, (place + step) % length * rows, from_right.shape[1], axis=1
+                ),
+                preferred_element_type=jnp.float32,
+            )
+        partial_value = partial_value + jnp.einsum(
+            "ikc,jkc->ijc",
+            from_left,
+            lax.dynamic_slice_in_dim(
+                right_diag, (place - step) % length * rows, from_left.shape[1], axis=1
+            ),
+            preferred_element_type=jnp.float32,
+        )
     tri = lax.psum_scatter(
         partial_value.astype(jnp.bfloat16), "ka", scatter_dimension=1, tiled=True
     ).astype(jnp.float32)

time: 424 us -> 437 us (1.031)
  waiting for transfers between devices: 335 us -> 260 us
  starting transfers between devices: 7.61 us -> 50.7 us
  local copies, waits for them, and re-layouts: 42.3 us -> 69.9 us
  matrix products: 16 us -> 33.5 us
    all_gather x1 -> x0, waiting for transfers between devices: 45.1 us -> none  [on_device(): left_rows = lax.all_gather(left, 'col', axis=1, tiled=True)]
    ppermute x0 -> x15, starting transfers between devices: none -> 42.9 us  [the longest x7 35.2 us: on_device(): from_right = lax.ppermute(from_right, 'col', backward)]
    all_gather x1, waiting for transfers between devices: 57.6 us -> 18.9 us  [on_device(): lax.all_gather(transpose_tiles(right, n), 'row', axis=1, tiled=True)]
    dynamic_slice x0 -> x17, local copies, waits for them, and re-layouts: none -> 36.4 us  [the longest x8 18.5 us: on_device(): lax.dynamic_slice_in_dim(right_diag, (place + step) % length * rows, from...]
    all_gather x2 -> x0, local copies, waits for them, and re-layouts: 30.5 us -> none  [the longest x1 15.2 us: on_device(): left_rows = lax.all_gather(left, 'col', axis=1, tiled=True)]
    dot_general x1 -> x16, matrix products: 9.18 us -> 25.7 us  [the longest x8 16.2 us: on_device(): jnp.einsum('ikc,jkc->ijc', from_left, lax.dynamic_slice_in_dim(right_diag...]
    ppermute x0 -> x15, local copies, waits for them, and re-layouts: none -> 15 us  [the longest x8 7.8 us: on_device(): from_left = lax.ppermute(from_left, 'col', ahead)]
    ppermute x0 -> x15, waiting for transfers between devices: none -> 11.3 us  [the longest x8 8.29 us: on_device(): from_left = lax.ppermute(from_left, 'col', ahead)]
  transfers between devices with their start and end apart: 8 -> 22, of which waited for: 8 -> 20; matrix products, arithmetic and copies ran while one was open for 6% -> 6% of each run, Pallas kernels for 0% -> 0%
where the time goes in v1:
time: 437 us; the launch traced here: 436 us
  waiting for transfers between devices  260 us (59%)
  local copies, waits for them, and re-layouts  69.9 us (16%)
  starting transfers between devices  50.7 us (12%)
  matrix products  33.5 us (8%)
  between operations  13.5 us (3%)
  other arithmetic  8.19 us (2%)
    all_gather x1, waiting for transfers between devices, on_device(): left_diag = lax.all_gather(left_half, 'ka', axis=1, tiled=True)  73.1 us
    all_gather x1, waiting for transfers between devices, on_device(): right_cols = lax.all_gather(right, 'row', axis=0, tiled=True)  58.5 us
    all_gather x1, waiting for transfers between devices, on_device(): lax.all_gather(transpose_tiles(left, n), 'col', axis=0, tiled=True)  53.4 us
    reduce_scatter x1, waiting for transfers between devices, on_device(): lax.psum_scatter(partial_value.astype(jnp.bfloat16), 'ka', scatter_dimens...  38.3 us
    ppermute x7, starting transfers between devices, on_device(): from_right = lax.ppermute(from_right, 'col', backward)  35.2 us
    all_gather x1, waiting for transfers between devices, on_device(): lax.all_gather(transpose_tiles(right, n), 'row', axis=1, tiled=True)  18.9 us
    dynamic_slice x8, local copies, waits for them, and re-layouts, on_device(): lax.dynamic_slice_in_dim(right_diag, (place + step) % length * rows, from...  18.5 us
    dynamic_slice x8, local copies, waits for them, and re-layouts, on_device(): lax.dynamic_slice_in_dim(right_diag, (place - step) % length * rows, from...  16.7 us
  transfers between devices with their start and end apart: 22, of which 20 were waited for; matrix products, arithmetic and copies ran while one was open for 6% of the time, Pallas kernels for 0%

profile of v1, /device:TPU:1, one launch (start us, length us, event | category | flops | bytes accessed | tf_op | source)
XLA Modules:
  0.0 435.9 jit_solution(8963251332249827258)
XLA Ops:
  11.4 4.5 %collective-permute-start = (bf16[32,16,128]{2,1,0:T(8,128)(2,1)S(1)}, bf16[32,16,128]{2,1,0:T(8,128)(2,1)S(1)}, u32[]{:S(2)}, u32[]{:S(2)}) collective-permute-start(bf16[32,16,128]{2,1,0:T(8,128)(2,1)S(1)} %get-tuple-element.24), channel_id=1, source_target_pairs={{0,0},{2,32},{4,64},{6,96},{8,128},{10,160},{12,192},{14,224},{16,... | collective-permute-start | bytes 393224 | tf_op jit(solution)/shard_map/ppermute | solution.py:38
  15.9 2.6 collective-permute-done
  19.2 5.1 %collective-permute-start.2 = (bf16[32,16,128]{2,1,0:T(8,128)(2,1)S(1)}, bf16[32,16,128]{2,1,0:T(8,128)(2,1)S(1)}, u32[]{:S(2)}, u32[]{:S(2)}) collective-permute-start(bf16[32,16,128]{2,1,0:T(8,128)(2,1)S(1)} %get-tuple-element.23), channel_id=1, source_target_pairs={{0,2},{2,4},{4,6},{6,8},{8,10},{10,12},{12,14},{14,16},{16,18},{18... | collective-permute-start | bytes 393224 | tf_op jit(solution)/shard_map/ppermute | solution.py:57
  24.4 4.2 collective-permute-done.2
  28.5 2.5 collective-permute-start.4
  32.7 11.8 %collective-permute-start.3 = (bf16[32,16,128]{2,1,0:T(8,128)(2,1)S(1)}, bf16[32,16,128]{2,1,0:T(8,128)(2,1)S(1)}, u32[]{:S(2)}, u32[]{:S(2)}) collective-permute-start(bf16[32,16,128]{2,1,0:T(8,128)(2,1)S(1)} %collective-permute-done.1), channel_id=1, source_target_pairs={{0,30},{2,0},{4,2},{6,4},{8,6},{10,8},{12,10},{14,12},{16,14},{18,... | collective-permute-start | bytes 393224 | tf_op jit(solution)/shard_map/ppermute | solution.py:59
  45.5 4.6 %collective-permute-start.5 = (bf16[32,16,128]{2,1,0:T(8,128)(2,1)S(1)}, bf16[32,16,128]{2,1,0:T(8,128)(2,1)S(1)}, u32[]{:S(2)}, u32[]{:S(2)}) collective-permute-start(bf16[32,16,128]{2,1,0:T(8,128)(2,1)S(1)} %collective-permute-done.3), channel_id=1, source_target_pairs={{0,30},{2,0},{4,2},{6,4},{8,6},{10,8},{12,10},{14,12},{16,14},{18,... | collective-permute-start | bytes 393224 | tf_op jit(solution)/shard_map/ppermute | solution.py:59
  51.1 4.6 %collective-permute-start.7 = (bf16[32,16,128]{2,1,0:T(8,128)(2,1)S(1)}, bf16[32,16,128]{2,1,0:T(8,128)(2,1)S(1)}, u32[]{:S(2)}, u32[]{:S(2)}) collective-permute-start(bf16[32,16,128]{2,1,0:T(8,128)(2,1)S(1)} %collective-permute-done.5), channel_id=1, source_target_pairs={{0,30},{2,0},{4,2},{6,4},{8,6},{10,8},{12,10},{14,12},{16,14},{18,... | collective-permute-start | bytes 393224 | tf_op jit(solution)/shard_map/ppermute | solution.py:59
  56.7 4.9 %collective-permute-start.9 = (bf16[32,16,128]{2,1,0:T(8,128)(2,1)S(1)}, bf16[32,16,128]{2,1,0:T(8,128)(2,1)S(1)}, u32[]{:S(2)}, u32[]{:S(2)}) collective-permute-start(bf16[32,16,128]{2,1,0:T(8,128)(2,1)S(1)} %collective-permute-done.7), channel_id=1, source_target_pairs={{0,30},{2,0},{4,2},{6,4},{8,6},{10,8},{12,10},{14,12},{16,14},{18,... | collective-permute-start | bytes 393224 | tf_op jit(solution)/shard_map/ppermute | solution.py:59
  62.6 4.6 %collective-permute-start.11 = (bf16[32,16,128]{2,1,0:T(8,128)(2,1)S(1)}, bf16[32,16,128]{2,1,0:T(8,128)(2,1)S(1)}, u32[]{:S(2)}, u32[]{:S(2)}) collective-permute-start(bf16[32,16,128]{2,1,0:T(8,128)(2,1)S(1)} %collective-permute-done.9), channel_id=1, source_target_pairs={{0,30},{2,0},{4,2},{6,4},{8,6},{10,8},{12,10},{14,12},{16,14},{18,... | collective-permute-start | bytes 393224 | tf_op jit(solution)/shard_map/ppermute | solution.py:59
  68.2 4.6 %collective-permute-start.13 = (bf16[32,16,128]{2,1,0:T(8,128)(2,1)S(1)}, bf16[32,16,128]{2,1,0:T(8,128)(2,1)S(1)}, u32[]{:S(2)}, u32[]{:S(2)}) collective-permute-start(bf16[32,16,128]{2,1,0:T(8,128)(2,1)S(1)} %collective-permute-done.11), channel_id=1, source_target_pairs={{0,30},{2,0},{4,2},{6,4},{8,6},{10,8},{12,10},{14,12},{16,14},{18,... | collective-permute-start | bytes 393224 | tf_op jit(solution)/shard_map/ppermute | solution.py:59
  89.6 18.9 %all-gather.5.cloned.1.call-done = bf16[32,256,128]{2,1,0:T(8,128)(2,1)} async-done(((bf16[32,16,128]{2,1,0:T(8,128)(2,1)}), bf16[32,256,128]{2,1,0:T(8,128)(2,1)}) %all-gather.5.cloned.1.call-update) | async-done | bytes 2097168 | tf_op jit(solution)/shard_map/all_gather | solution.py:44
  108.6 2.9 constant_dynamic-slice_fusion.14
  129.1 2.4 copy.148
  167.0 8.4 %fusion = bf16[32,32,128]{0,1,2:T(8,128)(2,1)} fusion(bf16[32,16,128]{0,1,2:T(8,128)(2,1)} %copy.168, bf16[32,16,128]{0,1,2:T(8,128)(2,1)S(1)} %copy.169, f32[128,32,32]{2,1,0:T(8,128)S(1)} %fusion.72, f32[128,32,32]{2,1,0:T(8,128)S(1)} %fusion.71, f32[128,32,32]{2,1,0:T(8,128)S(1)} %fusion.70, f32[128,32,32]{2,1,0:T(8,128)S(1)} %fusion.69, ...), kind=kOutput, calls=%fused_computation.1 | convolution fusion | flops 6291456 | bytes 8388608 | tf_op jit(solution)/shard_map/ikc,jkc->ijc/dot_general | solution.py:68
  177.1 38.3 %reduce-scatter.2.cloned.1.call-done = bf16[32,16,128]{0,1,2:T(8,128)(2,1)} async-done(((bf16[32,32,128]{0,1,2:T(8,128)(2,1)}), bf16[32,16,128]{0,1,2:T(8,128)(2,1)}) %reduce-scatter.2.cloned.1.call-update) | async-done | bytes 131088 | tf_op jit(solution)/shard_map/reduce_scatter | solution.py:76
  221.6 2.9 collective-permute-start.16
  224.5 3.4 collective-permute-done.16
  229.2 53.4 %all-gather.9.cloned.1.call-done = bf16[512,16,128]{2,1,0:T(8,128)(2,1)} async-done(((bf16[32,16,128]{2,1,0:T(8,128)(2,1)}), bf16[512,16,128]{2,1,0:T(8,128)(2,1)}) %all-gather.9.cloned.1.call-update) | async-done | bytes 2097168 | tf_op jit(solution)/shard_map/all_gather | solution.py:82
  282.6 4.9 %copy.175 = bf16[512,16,128]{0,1,2:T(8,128)(2,1)} copy(bf16[512,16,128]{2,1,0:T(8,128)(2,1)} %all-gather.9.cloned.1.call-done) | data formatting | bytes 4194304 | tf_op jit(solution)/shard_map/all_gather | solution.py:82
  288.8 58.5 %all-gather.7.cloned.1.call-done = bf16[512,16,128]{2,1,0:T(8,128)(2,1)} async-done(((bf16[32,16,128]{2,1,0:T(8,128)(2,1)}), bf16[512,16,128]{2,1,0:T(8,128)(2,1)}) %all-gather.7.cloned.1.call-update) | async-done | bytes 2097168 | tf_op jit(solution)/shard_map/all_gather | solution.py:81
  347.2 3.9 copy.176
  351.2 73.1 %all-gather.11.cloned.1.call-done = bf16[512,32,128]{0,1,2:T(8,128)(2,1)} async-done(((bf16[512,16,128]{0,1,2:T(8,128)(2,1)}), bf16[512,32,128]{0,1,2:T(8,128)(2,1)}) %all-gather.11.cloned.1.call-update) | async-done | bytes 4194320 | tf_op jit(solution)/shard_map/all_gather | solution.py:83
  424.2 3.4 fusion.57
  (177 shorter events, 93.7 us)
Async XLA Ops:
  6.5 102.0 %all-gather.5.cloned.1.call-start = ((), (), s32[]{:S(2)}) async-start(), calls=%async_computation.1 | async-start | bytes 2228224 | tf_op jit(solution)/shard_map/all_gather | solution.py:44
  9.9 66.0 %copy-start.25 = (f32[32,16]{1,0:T(8,128)}, f32[32,16]{1,0:T(8,128)S(1)}, u32[]{:S(2)}) copy-start(f32[32,16]{1,0:T(8,128)S(1)} %copy.137) | copy-start | bytes 6148
  11.4 7.1 %collective-permute-start = (bf16[32,16,128]{2,1,0:T(8,128)(2,1)S(1)}, bf16[32,16,128]{2,1,0:T(8,128)(2,1)S(1)}, u32[]{:S(2)}, u32[]{:S(2)}) collective-permute-start(bf16[32,16,128]{2,1,0:T(8,128)(2,1)S(1)} %get-tuple-element.24), channel_id=1, source_target_pairs={{0,0},{2,32},{4,64},{6,96},{8,128},{10,160},{12,192},{14,224},{16,... | collective-permute-start | bytes 393224 | tf_op jit(solution)/shard_map/ppermute | solution.py:38
  19.2 196.2 %reduce-scatter.2.cloned.1.call-start = ((), (), s32[]{:S(2)}) async-start(), calls=%async_computation.2 | async-start | bytes 1572864 | tf_op jit(solution)/shard_map/reduce_scatter | solution.py:76
  19.2 9.3 %collective-permute-start.2 = (bf16[32,16,128]{2,1,0:T(8,128)(2,1)S(1)}, bf16[32,16,128]{2,1,0:T(8,128)(2,1)S(1)}, u32[]{:S(2)}, u32[]{:S(2)}) collective-permute-start(bf16[32,16,128]{2,1,0:T(8,128)(2,1)S(1)} %get-tuple-element.23), channel_id=1, source_target_pairs={{0,2},{2,4},{4,6},{6,8},{8,10},{10,12},{12,14},{14,16},{16,18},{18... | collective-permute-start | bytes 393224 | tf_op jit(solution)/shard_map/ppermute | solution.py:57
  24.4 8.3 %collective-permute-start.1 = (bf16[32,16,128]{2,1,0:T(8,128)(2,1)S(1)}, bf16[32,16,128]{2,1,0:T(8,128)(2,1)S(1)}, u32[]{:S(2)}, u32[]{:S(2)}) collective-permute-start(bf16[32,16,128]{2,1,0:T(8,128)(2,1)S(1)} %get-tuple-element.23), channel_id=1, source_target_pairs={{0,30},{2,0},{4,2},{6,4},{8,6},{10,8},{12,10},{14,12},{16,14},{18,... | collective-permute-start | bytes 393224 | tf_op jit(solution)/shard_map/ppermute | solution.py:59
  28.5 16.8 %collective-permute-start.4 = (bf16[32,16,128]{2,1,0:T(8,128)(2,1)S(1)}, bf16[32,16,128]{2,1,0:T(8,128)(2,1)S(1)}, u32[]{:S(2)}, u32[]{:S(2)}) collective-permute-start(bf16[32,16,128]{2,1,0:T(8,128)(2,1)S(1)} %collective-permute-done.2), channel_id=1, source_target_pairs={{0,2},{2,4},{4,6},{6,8},{8,10},{10,12},{12,14},{14,16},{16,18},{18... | collective-permute-start | bytes 393224 | tf_op jit(solution)/shard_map/ppermute | solution.py:57
  32.7 12.8 %collective-permute-start.3 = (bf16[32,16,128]{2,1,0:T(8,128)(2,1)S(1)}, bf16[32,16,128]{2,1,0:T(8,128)(2,1)S(1)}, u32[]{:S(2)}, u32[]{:S(2)}) collective-permute-start(bf16[32,16,128]{2,1,0:T(8,128)(2,1)S(1)} %collective-permute-done.1), channel_id=1, source_target_pairs={{0,30},{2,0},{4,2},{6,4},{8,6},{10,8},{12,10},{14,12},{16,14},{18,... | collective-permute-start | bytes 393224 | tf_op jit(solution)/shard_map/ppermute | solution.py:59
  45.4 5.6 %collective-permute-start.6 = (bf16[32,16,128]{2,1,0:T(8,128)(2,1)S(1)}, bf16[32,16,128]{2,1,0:T(8,128)(2,1)S(1)}, u32[]{:S(2)}, u32[]{:S(2)}) collective-permute-start(bf16[32,16,128]{2,1,0:T(8,128)(2,1)S(1)} %collective-permute-done.4), channel_id=1, source_target_pairs={{0,2},{2,4},{4,6},{6,8},{8,10},{10,12},{12,14},{14,16},{16,18},{18... | collective-permute-start | bytes 393224 | tf_op jit(solution)/shard_map/ppermute | solution.py:57
  45.5 5.6 %collective-permute-start.5 = (bf16[32,16,128]{2,1,0:T(8,128)(2,1)S(1)}, bf16[32,16,128]{2,1,0:T(8,128)(2,1)S(1)}, u32[]{:S(2)}, u32[]{:S(2)}) collective-permute-start(bf16[32,16,128]{2,1,0:T(8,128)(2,1)S(1)} %collective-permute-done.3), channel_id=1, source_target_pairs={{0,30},{2,0},{4,2},{6,4},{8,6},{10,8},{12,10},{14,12},{16,14},{18,... | collective-permute-start | bytes 393224 | tf_op jit(solution)/shard_map/ppermute | solution.py:59
  51.0 5.6 %collective-permute-start.8 = (bf16[32,16,128]{2,1,0:T(8,128)(2,1)S(1)}, bf16[32,16,128]{2,1,0:T(8,128)(2,1)S(1)}, u32[]{:S(2)}, u32[]{:S(2)}) collective-permute-start(bf16[32,16,128]{2,1,0:T(8,128)(2,1)S(1)} %collective-permute-done.6), channel_id=1, source_target_pairs={{0,2},{2,4},{4,6},{6,8},{8,10},{10,12},{12,14},{14,16},{16,18},{18... | collective-permute-start | bytes 393224 | tf_op jit(solution)/shard_map/ppermute | solution.py:57
  51.1 5.6 %collective-permute-start.7 = (bf16[32,16,128]{2,1,0:T(8,128)(2,1)S(1)}, bf16[32,16,128]{2,1,0:T(8,128)(2,1)S(1)}, u32[]{:S(2)}, u32[]{:S(2)}) collective-permute-start(bf16[32,16,128]{2,1,0:T(8,128)(2,1)S(1)} %collective-permute-done.5), channel_id=1, source_target_pairs={{0,30},{2,0},{4,2},{6,4},{8,6},{10,8},{12,10},{14,12},{16,14},{18,... | collective-permute-start | bytes 393224 | tf_op jit(solution)/shard_map/ppermute | solution.py:59
  56.6 5.6 %collective-permute-start.10 = (bf16[32,16,128]{2,1,0:T(8,128)(2,1)S(1)}, bf16[32,16,128]{2,1,0:T(8,128)(2,1)S(1)}, u32[]{:S(2)}, u32[]{:S(2)}) collective-permute-start(bf16[32,16,128]{2,1,0:T(8,128)(2,1)S(1)} %collective-permute-done.8), channel_id=1, source_target_pairs={{0,2},{2,4},{4,6},{6,8},{8,10},{10,12},{12,14},{14,16},{16,18},{18... | collective-permute-start | bytes 393224 | tf_op jit(solution)/shard_map/ppermute | solution.py:57
  56.7 5.9 %collective-permute-start.9 = (bf16[32,16,128]{2,1,0:T(8,128)(2,1)S(1)}, bf16[32,16,128]{2,1,0:T(8,128)(2,1)S(1)}, u32[]{:S(2)}, u32[]{:S(2)}) collective-permute-start(bf16[32,16,128]{2,1,0:T(8,128)(2,1)S(1)} %collective-permute-done.7), channel_id=1, source_target_pairs={{0,30},{2,0},{4,2},{6,4},{8,6},{10,8},{12,10},{14,12},{16,14},{18,... | collective-permute-start | bytes 393224 | tf_op jit(solution)/shard_map/ppermute | solution.py:59
  62.2 5.6 %collective-permute-start.12 = (bf16[32,16,128]{2,1,0:T(8,128)(2,1)S(1)}, bf16[32,16,128]{2,1,0:T(8,128)(2,1)S(1)}, u32[]{:S(2)}, u32[]{:S(2)}) collective-permute-start(bf16[32,16,128]{2,1,0:T(8,128)(2,1)S(1)} %collective-permute-done.10), channel_id=1, source_target_pairs={{0,2},{2,4},{4,6},{6,8},{8,10},{10,12},{12,14},{14,16},{16,18},{18... | collective-permute-start | bytes 393224 | tf_op jit(solution)/shard_map/ppermute | solution.py:57
  62.6 5.6 %collective-permute-start.11 = (bf16[32,16,128]{2,1,0:T(8,128)(2,1)S(1)}, bf16[32,16,128]{2,1,0:T(8,128)(2,1)S(1)}, u32[]{:S(2)}, u32[]{:S(2)}) collective-permute-start(bf16[32,16,128]{2,1,0:T(8,128)(2,1)S(1)} %collective-permute-done.9), channel_id=1, source_target_pairs={{0,30},{2,0},{4,2},{6,4},{8,6},{10,8},{12,10},{14,12},{16,14},{18,... | collective-permute-start | bytes 393224 | tf_op jit(solution)/shard_map/ppermute | solution.py:59
  67.8 5.6 %collective-permute-start.14 = (bf16[32,16,128]{2,1,0:T(8,128)(2,1)S(1)}, bf16[32,16,128]{2,1,0:T(8,128)(2,1)S(1)}, u32[]{:S(2)}, u32[]{:S(2)}) collective-permute-start(bf16[32,16,128]{2,1,0:T(8,128)(2,1)S(1)} %collective-permute-done.12), channel_id=1, source_target_pairs={{0,2},{2,4},{4,6},{6,8},{8,10},{10,12},{12,14},{14,16},{16,18},{18... | collective-permute-start | bytes 393224 | tf_op jit(solution)/shard_map/ppermute | solution.py:57
  68.2 18.7 %collective-permute-start.13 = (bf16[32,16,128]{2,1,0:T(8,128)(2,1)S(1)}, bf16[32,16,128]{2,1,0:T(8,128)(2,1)S(1)}, u32[]{:S(2)}, u32[]{:S(2)}) collective-permute-start(bf16[32,16,128]{2,1,0:T(8,128)(2,1)S(1)} %collective-permute-done.11), channel_id=1, source_target_pairs={{0,30},{2,0},{4,2},{6,4},{8,6},{10,8},{12,10},{14,12},{16,14},{18,... | collective-permute-start | bytes 393224 | tf_op jit(solution)/shard_map/ppermute | solution.py:59
  73.4 14.8 %collective-permute-start.15 = (bf16[32,16,128]{2,1,0:T(8,128)(2,1)S(1)}, bf16[32,16,128]{2,1,0:T(8,128)(2,1)}, u32[]{:S(2)}, u32[]{:S(2)}) collective-permute-start(bf16[32,16,128]{2,1,0:T(8,128)(2,1)S(1)} %collective-permute-done.14), channel_id=1, source_target_pairs={{0,2},{2,4},{4,6},{6,8},{8,10},{10,12},{12,14},{14,16},{16,18},{18... | collective-permute-start | bytes 393224 | tf_op jit(solution)/shard_map/ppermute | solution.py:57
  175.5 44.0 %copy-start.23 = (bf16[32,16,128]{2,1,0:T(8,128)(2,1)S(1)}, bf16[32,16,128]{2,1,0:T(8,128)(2,1)}, u32[]{:S(2)}) copy-start(bf16[32,16,128]{2,1,0:T(8,128)(2,1)} %param.5) | copy-start | bytes 393220
  175.5 107.1 %all-gather.9.cloned.1.call-start = ((), (), s32[]{:S(2)}) async-start(), calls=%async_computation.4 | async-start | bytes 2228224 | tf_op jit(solution)/shard_map/all_gather | solution.py:82
  221.6 6.3 %collective-permute-start.16 = (bf16[32,16,128]{2,1,0:T(8,128)(2,1)S(1)}, bf16[32,16,128]{2,1,0:T(8,128)(2,1)S(1)}, u32[]{:S(2)}, u32[]{:S(2)}) collective-permute-start(bf16[32,16,128]{2,1,0:T(8,128)(2,1)S(1)} %get-tuple-element.21), channel_id=1, source_target_pairs={{0,0},{2,32},{4,64},{6,96},{8,128},{10,160},{12,192},{14,224},{16,... | collective-permute-start | bytes 393224 | tf_op jit(solution)/shard_map/ppermute | solution.py:38
  228.6 118.7 %all-gather.7.cloned.1.call-start = ((), (), s32[]{:S(2)}) async-start(), calls=%async_computation.3 | async-start | bytes 2228224 | tf_op jit(solution)/shard_map/all_gather | solution.py:81
  229.2 195.1 %all-gather.11.cloned.1.call-start = ((), (), s32[]{:S(2)}) async-start(), calls=%async_computation.5 | async-start | bytes 6291456 | tf_op jit(solution)/shard_map/all_gather | solution.py:83
  (30 other events, 127.9 us)
Sparse Core Ops, SparseCore 0:
  19.3 89.2 all-gather.4
  175.6 39.6 reduce-scatter.1
  228.7 53.9 all-gather.8
  284.6 62.6 all-gather.6
  349.2 75.0 all-gather.10
